TPU v7x, 128 devices: a whole 4x4x4 slice. The times are simulated.
128 devices in a mesh: inline: 16 (over z, x), crosslin: 8 (over y, core).
Axes of the slice: x: 4, y: 4, z: 4, core: 2. Of those that a mesh axis runs over, the one named last changes fastest.
Arguments:
- grid_feat: bfloat16 [262144, 512], P(('inline', 'crosslin')), may hold values from -68 to 68
- cotangent: bfloat16 [262144, 512], P(('inline', 'crosslin')), may hold values from -6 to 6
- trace_feat: bfloat16 [16384, 512], P(('inline', 'crosslin')), may hold values from -6 to 6
- trace_dest: int32 [16384, 2], P(('inline', 'crosslin')), may hold values from 0 to 127, all different within a row; in each aligned block of 128 rows (0 to 127, 128 to 255, ...) at most 4 rows name the same one
- query_weight: bfloat16 [512, 512], replicated, may hold values from -0.25 to 0.25
- key_weight: bfloat16 [512, 512], replicated, may hold values from -0.25 to 0.25
- value_weight: bfloat16 [512, 512], replicated, may hold values from -0.25 to 0.25
- output_weight: bfloat16 [512, 512], replicated, may hold values from -0.25 to 0.25
Outputs:
- grad_grid: bfloat16 [262144, 512], P(('inline', 'crosslin'))
- grad_trace: float32 [16384, 512], P(('inline', 'crosslin'))
- grad_query: float32 [512, 512], replicated
- grad_key: float32 [512, 512], replicated
- grad_value: float32 [512, 512], replicated
- grad_output: float32 [512, 512], replicated
Inputs may be any that keep to these rules, and one draw needn't show every extreme that they name: `trace_dest`: in the 128 rows of one device no tile is named by more than 4 rows, a bound that some block reaches; a row names 2 different tiles; every tile is named by some row.
All inputs are finite; a program needn't handle non-finite values.
Results may differ from a plain program's by a relative error of at most 0.013.
The roundings to bfloat16 on the way count: a program that leaves them out, or rounds other values in their place, can miss the bound.
Values may be sent and summed in bfloat16 or wider, within the bound.
No kernel may reach another device: no remote copies, remote signals or barrier semaphores. Data moves between devices by JAX's collectives and lax.ppermute only.
A program may use at most 64 MiB of HBM per device.

v0:
```python
import jax
import jax.numpy as jnp
from jax import lax
from jax.sharding import PartitionSpec as P

HEADS = 8
TOP = 2


def slot_table(targets, tile_count, capacity):
    tile_ids = jnp.arange(tile_count, dtype=jnp.int32)
    named = jnp.any(targets[:, :, None] == tile_ids[None, None, :], axis=1)
    position = jnp.cumsum(named.astype(jnp.int32), axis=0) - 1
    places = jnp.arange(capacity, dtype=jnp.int32)
    chosen = named.T[:, None, :] & (position.T[:, None, :] == places[None, :, None])
    return (chosen, jnp.sum(named.astype(jnp.int32), axis=0))


def tile_grad(grid_rows, upstream, query_weight, output_weight, key_tile, value_tile, live_slots):
    model_width = grid_rows.shape[1]
    head_size = model_width // HEADS
    factor = head_size ** (-0.5)
    queries = jnp.dot(grid_rows, query_weight, preferred_element_type=jnp.float32).astype(
        jnp.bfloat16
    )
    out_grad = jnp.dot(upstream, output_weight.T, preferred_element_type=jnp.float32).astype(
        jnp.bfloat16
    )

    def one_head(head_index):
        offset = head_index * head_size
        query_head = lax.dynamic_slice_in_dim(queries, offset, head_size, 1)
        key_head = lax.dynamic_slice_in_dim(key_tile, offset, head_size, 1)
        value_head = lax.dynamic_slice_in_dim(value_tile, offset, head_size, 1)
        grad_head = lax.dynamic_slice_in_dim(out_grad, offset, head_size, 1)
        scores = jnp.dot(query_head, key_head.T, preferred_element_type=jnp.float32) * factor
        scores = jnp.where(live_slots[None, :], scores, -1e30)
        row_peak = jnp.max(scores, axis=1, keepdims=True)
        raised = jnp.exp(scores - row_peak)
        attention = raised / jnp.sum(raised, axis=1, keepdims=True)
        prob_half = attention.astype(jnp.bfloat16)
        head_out = jnp.dot(prob_half, value_head, preferred_element_type=jnp.float32).astype(
            jnp.bfloat16
        )
        prob_grad = jnp.dot(grad_head, value_head.T, preferred_element_type=jnp.float32)
        correction = jnp.sum(attention * prob_grad, axis=1, keepdims=True)
        score_grad = (attention * (prob_grad - correction) * factor).astype(jnp.bfloat16)
        query_grad = jnp.dot(score_grad, key_head, preferred_element_type=jnp.float32).astype(
            jnp.bfloat16
        )
        key_grad = jnp.dot(score_grad.T, query_head, preferred_element_type=jnp.float32).astype(
            jnp.bfloat16
        )
        value_grad = jnp.dot(prob_half.T, grad_head, preferred_element_type=jnp.float32).astype(
            jnp.bfloat16
        )
        return (head_out, query_grad, key_grad, value_grad)

    def join_heads(stacked):
        return jnp.transpose(stacked, (1, 0, 2)).reshape(stacked.shape[1], model_width)

    stacked = lax.map(one_head, jnp.arange(HEADS, dtype=jnp.int32))
    attn_out, query_grad, key_grad, value_grad = [
        join_heads(stacked_part) for stacked_part in stacked
    ]
    part_output = jnp.dot(attn_out.T, upstream, preferred_element_type=jnp.float32)
    grad_grid = jnp.dot(query_grad, query_weight.T, preferred_element_type=jnp.float32).astype(
        jnp.bfloat16
    )
    part_query = jnp.dot(grid_rows.T, query_grad, preferred_element_type=jnp.float32)
    return (grad_grid, key_grad, value_grad, part_output, part_query)


def send_slots(outgoing):
    arrived = lax.all_to_all(
        outgoing, ("inline", "crosslin"), split_axis=0, concat_axis=0, tiled=True
    )
    return arrived


def send_back(returned):
    result_rows = lax.all_to_all(
        returned, ("inline", "crosslin"), split_axis=0, concat_axis=0, tiled=True
    )
    return result_rows


def on_device(
    grid_feat,
    cotangent,
    trace_feat,
    trace_dest,
    query_weight,
    key_weight,
    value_weight,
    output_weight,
):
    tile_count = lax.axis_size("inline") * lax.axis_size("crosslin")
    trace_rows = trace_feat.shape[0]
    model_width = trace_feat.shape[1]
    capacity = 2 * trace_rows * TOP // tile_count
    chosen, counts = slot_table(trace_dest, tile_count, capacity)
    picker = chosen.astype(jnp.bfloat16)
    key_rows = jnp.dot(trace_feat, key_weight, preferred_element_type=jnp.float32).astype(
        jnp.bfloat16
    )
    value_rows = jnp.dot(trace_feat, value_weight, preferred_element_type=jnp.float32).astype(
        jnp.bfloat16
    )
    flag = jnp.ones((trace_rows, 128), jnp.bfloat16)
    packed = jnp.concatenate([key_rows, value_rows, trace_feat, flag], axis=1)
    outgoing = jnp.einsum("tjr,rd->tjd", picker, packed, preferred_element_type=jnp.float32).astype(
        jnp.bfloat16
    )
    arrived = send_slots(outgoing)
    arrived = arrived.reshape(tile_count * capacity, packed.shape[1])
    key_tile = arrived[:, :model_width]
    value_tile = arrived[:, model_width : 2 * model_width]
    feat_tile = arrived[:, 2 * model_width : 3 * model_width]
    live_slots = arrived[:, 3 * model_width] > 0.5
    grad_grid, key_grad, value_grad, part_output, part_query = tile_grad(
        grid_feat, cotangent, query_weight, output_weight, key_tile, value_tile, live_slots
    )
    part_key = jnp.dot(feat_tile.T, key_grad, preferred_element_type=jnp.float32)
    part_value = jnp.dot(feat_tile.T, value_grad, preferred_element_type=jnp.float32)
    grad_query, grad_key, grad_value, grad_output = lax.psum(
        (part_query, part_key, part_value, part_output), ("inline", "crosslin")
    )
    slot_trace = jnp.dot(key_grad, key_weight.T, preferred_element_type=jnp.float32)
    slot_trace = slot_trace + jnp.dot(
        value_grad, value_weight.T, preferred_element_type=jnp.float32
    )
    slot_trace = slot_trace.astype(jnp.bfloat16).reshape(tile_count, capacity, model_width)
    returned = send_back(slot_trace)
    grad_trace = jnp.einsum("tjr,tje->re", picker, returned, preferred_element_type=jnp.float32)
    return (grad_grid, grad_trace, grad_query, grad_key, grad_value, grad_output)


def solution(mesh):
    in_specs = (
        P(("inline", "crosslin"), None),
        P(("inline", "crosslin"), None),
        P(("inline", "crosslin"), None),
        P(("inline", "crosslin"), None),
        P(),
        P(),
        P(),
        P(),
    )
    out_specs = (
        P(("inline", "crosslin"), None),
        P(("inline", "crosslin"), None),
        P(),
        P(),
        P(),
        P(),
    )
    return jax.shard_map(
        on_device, mesh=mesh, in_specs=in_specs, out_specs=out_specs, check_vma=False
    )
```

profile of v0, /device:TPU:1, one launch (start us, length us, event | category | flops | bytes accessed | tf_op | source)
XLA Modules:
  0.0 360.5 jit_solution(8484255130443011278)
XLA Ops:
  12.6 2.5 copy.29
  15.1 11.9 %all-to-all-start = ((bf16[128,4,1664]{2,1,0:T(4,128)(2,1)}), bf16[128,4,1664]{2,1,0:T(4,128)(2,1)}, u32[]{:S(2)}, u32[]{:S(2)}) async-start(bf16[128,4,1664]{2,1,0:T(4,128)(2,1)} %copy.29), calls=%async_computation | async-start | bytes 3407872 | tf_op jit(solution)/shard_map/all_to_all | solution.py:75
  27.1 4.2 %convolution_convert_fusion.5 = bf16[2048,512]{1,0:T(8,128)(2,1)} fusion(bf16[2048,512]{1,0:T(8,128)(2,1)} %param.11, bf16[512,512]{1,0:T(8,128)(2,1)S(1)} %copy-done.9), kind=kOutput, calls=%fused_computation.38 | convolution fusion | flops 1074790400 | bytes 4718592 | tf_op jit(solution)/shard_map/dot_general | solution.py:26
  31.4 2.6 convolution_convert_fusion.6
  34.0 18.7 %all-to-all-done = bf16[128,4,1664]{2,1,0:T(4,128)(2,1)} async-done(((bf16[128,4,1664]{2,1,0:T(4,128)(2,1)}), bf16[128,4,1664]{2,1,0:T(4,128)(2,1)}, u32[]{:S(2)}, u32[]{:S(2)}) %all-to-all-start) | async-done | bytes 1703968 | tf_op jit(solution)/shard_map/all_to_all | solution.py:75
  52.7 3.8 %reshape.41 = bf16[512,1664]{1,0:T(8,128)(2,1)} reshape(bf16[128,4,1664]{2,1,0:T(4,128)(2,1)} %all-to-all-done) | data formatting | bytes 3407872 | tf_op jit(solution)/shard_map/reshape | solution.py:116
  56.5 2.1 fusion.52
  59.7 121.5 %while.16 = (s32[]{:T(128)}, bf16[8,2048,64]{1,2,0:T(8,128)(2,1)}, bf16[8,2048,64]{1,2,0:T(8,128)(2,1)}, bf16[8,512,64]{1,2,0:T(8,128)(2,1)}, bf16[8,512,64]{1,2...) while((s32[]{:T(128)}, bf16[8,2048,64]{1,2,0:T(8,128)(2,1)}, ...), condition=%wide.region_6.7_spmd, body=%wide.region_2.6_spmd.sunk | while | flops 838133760 | bytes 53721872 | solution.py:62
  70.3 2.6 fusion.103
  72.9 1.9 fusion.101
  85.5 2.6 fusion.103
  100.7 2.6 fusion.103
  115.9 2.6 fusion.103
  118.5 1.9 fusion.101
  131.1 2.6 fusion.103
  133.7 1.9 fusion.101
  146.3 2.6 fusion.103
  148.9 1.9 fusion.101
  161.5 2.6 fusion.103
  164.1 1.9 fusion.101
  176.7 2.6 fusion.103
  179.3 1.9 fusion.101
  181.2 2.6 fusion.33
  183.9 2.5 fusion.35
  186.4 2.2 convolution_bitcast_fusion
  188.6 3.8 %fusion.54 = f32[512,512]{1,0:T(8,128)} fusion(bf16[2048,512]{0,1:T(8,128)(2,1)} %bitcast.20, bf16[2048,512]{1,0:T(8,128)(2,1)S(1)} %copy-done.7), kind=kOutput, calls=%fused_computation.72 | convolution fusion | flops 1073741824 | bytes 5242880 | tf_op jit(solution)/shard_map/dot_general | solution.py:66
  196.5 4.9 %all-to-all-start.1 = ((bf16[128,4,512]{2,1,0:T(4,128)(2,1)}), bf16[128,4,512]{2,1,0:T(4,128)(2,1)S(1)}, u32[]{:S(2)}, u32[]{:S(2)}) async-start(bf16[128,4,512]{2,1,0:T(4,128)(2,1)} %reshape.45), calls=%async_computation.1 | async-start | bytes 1048576 | tf_op jit(solution)/shard_map/all_to_all | solution.py:82
  201.4 4.4 %convolution_convert_fusion.4 = bf16[2048,512]{1,0:T(8,128)(2,1)} fusion(bf16[2048,512]{0,1:T(8,128)(2,1)} %bitcast.81, bf16[512,512]{1,0:T(8,128)(2,1)} %param.14), kind=kOutput, calls=%fused_computation.37 | convolution fusion | flops 1074790400 | bytes 4718592 | tf_op jit(solution)/shard_map/dot_general | solution.py:67
  205.7 10.1 %all-to-all-done.1 = bf16[128,4,512]{2,1,0:T(4,128)(2,1)S(1)} async-done(((bf16[128,4,512]{2,1,0:T(4,128)(2,1)}), bf16[128,4,512]{2,1,0:T(4,128)(2,1)S(1)}, u32[]{:S(2)}, u32[]{:S(2)}) %all-to-all-start.1) | async-done | bytes 524320 | tf_op jit(solution)/shard_map/all_to_all | solution.py:82
  216.8 129.9 %all-reduce.3.cloned.1.call-done = (f32[512,512]{0,1:T(8,128)}, f32[512,512]{1,0:T(8,128)}, f32[512,512]{1,0:T(8,128)}, f32[512,512]{1,0:T(8,128)}) async-done(((f32[512,512]{0,1:T(8,128)}, f32[512,512]{1,0:T(8,128)}, f32[512,512]{1,0:T(8,128)}, f32[512,512]{1,0:T(8,128)}), (f32[512,512]{0,1:T(8,128)}, f32[512,512]{1,0:T(8,128)}, f32[512,512]{1,0:T(8,128)}, ...) | async-done | bytes 4194320 | tf_op jit(solution)/shard_map/psum | solution.py:126
  346.7 2.5 copy.31
  349.3 2.4 copy.58
  (133 shorter events, 96.8 us)
Async XLA Ops:
  7.2 24.2 %copy-start = (bf16[2048,512]{1,0:T(8,128)(2,1)S(1)}, bf16[2048,512]{1,0:T(8,128)(2,1)}, u32[]{:S(2)}) copy-start(bf16[2048,512]{1,0:T(8,128)(2,1)} %param.10) | copy-start | bytes 6291460
  15.1 12.0 %copy-start.9 = (bf16[512,512]{1,0:T(8,128)(2,1)S(1)}, bf16[512,512]{1,0:T(8,128)(2,1)}, u32[]{:S(2)}) copy-start(bf16[512,512]{1,0:T(8,128)(2,1)} %param.17) | copy-start | bytes 1572868
  15.1 37.6 %all-to-all-start = ((bf16[128,4,1664]{2,1,0:T(4,128)(2,1)}), bf16[128,4,1664]{2,1,0:T(4,128)(2,1)}, u32[]{:S(2)}, u32[]{:S(2)}) async-start(bf16[128,4,1664]{2,1,0:T(4,128)(2,1)} %copy.29), calls=%async_computation | async-start | bytes 3407872 | tf_op jit(solution)/shard_map/all_to_all | solution.py:75
  27.0 319.7 %all-reduce.3.cloned.1.call-start = ((), (), s32[]{:S(2)}) async-start(), calls=%async_computation.2 | async-start | bytes 8388608 | tf_op jit(solution)/shard_map/psum | solution.py:126
  27.1 4.3 %copy-start.10 = (bf16[512,512]{1,0:T(8,128)(2,1)S(1)}, bf16[512,512]{1,0:T(8,128)(2,1)}, u32[]{:S(2)}) copy-start(bf16[512,512]{1,0:T(8,128)(2,1)} %param.14) | copy-start | bytes 1572868
  62.8 1.0 copy-start.6
  62.8 1.8 copy-start.11
  78.0 1.0 copy-start.6
  78.0 1.8 copy-start.11
  93.2 1.0 copy-start.6
  93.2 1.8 copy-start.11
  108.4 1.0 copy-start.6
  108.4 1.8 copy-start.11
  123.6 1.0 copy-start.6
  123.6 1.8 copy-start.11
  138.7 1.0 copy-start.6
  138.8 1.8 copy-start.11
  153.9 1.0 copy-start.6
  153.9 1.8 copy-start.11
  169.1 1.0 copy-start.6
  169.1 1.8 copy-start.11
  181.2 2.7 copy-start.3
  181.2 5.2 %copy-start.8 = (bf16[8,2048,64]{1,2,0:T(8,128)(2,1)S(1)}, bf16[8,2048,64]{1,2,0:T(8,128)(2,1)}, u32[]{:S(2)}) copy-start(bf16[8,2048,64]{1,2,0:T(8,128)(2,1)} %get-tuple-element.66) | copy-start | bytes 6291460
  186.4 2.2 copy-start.7
  192.4 1.0 copy-start.2
  193.4 1.6 copy-start.1
  196.5 19.3 %all-to-all-start.1 = ((bf16[128,4,512]{2,1,0:T(4,128)(2,1)}), bf16[128,4,512]{2,1,0:T(4,128)(2,1)S(1)}, u32[]{:S(2)}, u32[]{:S(2)}) async-start(bf16[128,4,512]{2,1,0:T(4,128)(2,1)} %reshape.45), calls=%async_computation.1 | async-start | bytes 1048576 | tf_op jit(solution)/shard_map/all_to_all | solution.py:82
  349.3 2.4 copy-start.5
  349.3 3.4 copy-start.4
Sparse Core Ops, SparseCore 0:
  192.5 154.1 all-reduce.2
where the time goes:
time: 362 us; the launch traced here: 360 us
  waiting for transfers between devices  159 us (44%)
  matrix products  114 us (31%)
  local copies, waits for them, and re-layouts  28.8 us (8%)
  other arithmetic  22.6 us (6%)
  starting transfers between devices  16.8 us (5%)
  between operations  14.2 us (4%)
  loops' own time  5.71 us (2%)
    psum x1, waiting for transfers between devices, on_device(): lax.psum((part_query, part_key, part_value, part_output), ('inline', 'cro...  130 us
    dot_general x8, matrix products, one_head(): jnp.dot(score_grad.T, query_head, preferred_element_type=jnp.float32)  21 us
    all_to_all x1, waiting for transfers between devices, send_slots(): lax.all_to_all(outgoing, ('inline', 'crosslin'), split_axis=0, concat_axi...  18.7 us
    dot_general x8, matrix products, one_head(): jnp.dot(prob_half, value_head, preferred_element_type=jnp.float32)  15.4 us
    dot_general x8, matrix products, one_head(): jnp.dot(query_head, key_head.T, preferred_element_type=jnp.float32) * factor  14.8 us
    convert_element_type x8, other arithmetic, one_head(): (attention * (prob_grad - correction) * factor).astype(jnp.bfloat16)  13.3 us
    all_to_all x1, starting transfers between devices, send_slots(): lax.all_to_all(outgoing, ('inline', 'crosslin'), split_axis=0, concat_axi...  11.9 us
    dot_general x8, matrix products, one_head(): jnp.dot(grad_head, value_head.T, preferred_element_type=jnp.float32)  11.7 us
  transfers between devices with their start and end apart: 3, of which 3 were waited for; matrix products, arithmetic and copies ran while one was open for 4% of the time, Pallas kernels for 0%

commit v1 on v0

--- a/solution.py
+++ b/solution.py
@@ -124,7 +124,7 @@
     part_key = jnp.dot(feat_tile.T, key_grad, preferred_element_type=jnp.float32)
     part_value = jnp.dot(feat_tile.T, value_grad, preferred_element_type=jnp.float32)
     grad_query, grad_key, grad_value, grad_output = lax.psum(
-        (part_query, part_key, part_value, part_output), ("inline", "crosslin")
+        lax.psum((part_query, part_key, part_value, part_output), "inline"), "crosslin"
     )
     slot_trace = jnp.dot(key_grad, key_weight.T, preferred_element_type=jnp.float32)
     slot_trace = slot_trace + jnp.dot(

time: 362 us -> 388 us (1.072)
  waiting for transfers between devices: 159 us -> 180 us
    psum x1 -> x2, waiting for transfers between devices: 130 us -> 152 us  [the longest x1 100 us: on_device(): lax.psum((part_query, part_key, part_value, part_output), 'inline')]
  transfers between devices with their start and end apart: 3 -> 4, of which waited for: 3 -> 4; matrix products, arithmetic and copies ran while one was open for 4% -> 4% of each run, Pallas kernels for 0% -> 0%
where the time goes in v1:
time: 388 us; the launch traced here: 385 us
  waiting for transfers between devices  180 us (46%)
  matrix products  114 us (29%)
  local copies, waits for them, and re-layouts  28.8 us (7%)
  other arithmetic  22.6 us (6%)
  starting transfers between devices  20 us (5%)
  between operations  14.2 us (4%)
  loops' own time  5.71 us (1%)
    psum x1, waiting for transfers between devices, on_device(): lax.psum((part_query, part_key, part_value, part_output), 'inline')  100 us
    psum x1, waiting for transfers between devices, on_device(): lax.psum(lax.psum((part_query, part_key, part_value, part_output), 'inlin...  52.4 us
    dot_general x8, matrix products, one_head(): jnp.dot(score_grad.T, query_head, preferred_element_type=jnp.float32)  21 us
    all_to_all x1, waiting for transfers between devices, send_slots(): lax.all_to_all(outgoing, ('inline', 'crosslin'), split_axis=0, concat_axi...  18.7 us
    dot_general x8, matrix products, one_head(): jnp.dot(prob_half, value_head, preferred_element_type=jnp.float32)  15.4 us
    dot_general x8, matrix products, one_head(): jnp.dot(query_head, key_head.T, preferred_element_type=jnp.float32) * factor  14.8 us
    convert_element_type x8, other arithmetic, one_head(): (attention * (prob_grad - correction) * factor).astype(jnp.bfloat16)  13.3 us
    all_to_all x1, starting transfers between devices, send_slots(): lax.all_to_all(outgoing, ('inline', 'crosslin'), split_axis=0, concat_axi...  11.9 us
  transfers between devices with their start and end apart: 4, of which 4 were waited for; matrix products, arithmetic and copies ran while one was open for 4% of the time, Pallas kernels for 0%

profile of v1, /device:TPU:1, one launch (start us, length us, event | category | flops | bytes accessed | tf_op | source)
XLA Modules:
  0.0 385.3 jit_solution(4884145974704308268)
XLA Ops:
  12.6 2.5 copy.29
  15.1 11.9 %all-to-all-start = ((bf16[128,4,1664]{2,1,0:T(4,128)(2,1)}), bf16[128,4,1664]{2,1,0:T(4,128)(2,1)}, u32[]{:S(2)}, u32[]{:S(2)}) async-start(bf16[128,4,1664]{2,1,0:T(4,128)(2,1)} %copy.29), calls=%async_computation | async-start | bytes 3407872 | tf_op jit(solution)/shard_map/all_to_all | solution.py:75
  27.1 4.2 %convolution_convert_fusion.5 = bf16[2048,512]{1,0:T(8,128)(2,1)} fusion(bf16[2048,512]{1,0:T(8,128)(2,1)} %param.11, bf16[512,512]{1,0:T(8,128)(2,1)S(1)} %copy-done.9), kind=kOutput, calls=%fused_computation.38 | convolution fusion | flops 1074790400 | bytes 4718592 | tf_op jit(solution)/shard_map/dot_general | solution.py:26
  31.4 2.6 convolution_convert_fusion.6
  34.0 18.7 %all-to-all-done = bf16[128,4,1664]{2,1,0:T(4,128)(2,1)} async-done(((bf16[128,4,1664]{2,1,0:T(4,128)(2,1)}), bf16[128,4,1664]{2,1,0:T(4,128)(2,1)}, u32[]{:S(2)}, u32[]{:S(2)}) %all-to-all-start) | async-done | bytes 1703968 | tf_op jit(solution)/shard_map/all_to_all | solution.py:75
  52.7 3.8 reshape.41
  56.5 2.1 fusion.52
  59.7 121.6 %while.16 = (s32[]{:T(128)}, bf16[8,2048,64]{1,2,0:T(8,128)(2,1)}, bf16[8,2048,64]{1,2,0:T(8,128)(2,1)}, bf16[8,512,64]{1,2,0:T(8,128)(2,1)}, bf16[8,512,64]{1,2...) while((s32[]{:T(128)}, bf16[8,2048,64]{1,2,0:T(8,128)(2,1)}, ...), condition=%wide.region_6.7_spmd, body=%wide.region_2.6_spmd.sunk | while | flops 838133760 | bytes 53721872 | solution.py:62
  70.3 2.6 fusion.103
  73.0 1.9 fusion.101
  85.5 2.6 fusion.103
  88.2 1.9 fusion.101
  100.7 2.6 fusion.103
  116.0 2.6 fusion.103
  131.2 2.6 fusion.103
  146.4 2.6 fusion.103
  149.0 1.9 fusion.101
  161.5 2.6 fusion.103
  164.2 1.9 fusion.101
  176.7 2.6 fusion.103
  179.4 1.9 fusion.101
  181.3 2.6 fusion.33
  183.9 2.5 fusion.35
  186.4 2.2 convolution_bitcast_fusion
  188.7 3.8 fusion.54
  192.5 100.0 %all-reduce.5.cloned.1.call-done = (f32[512,512]{0,1:T(8,128)}, f32[512,512]{1,0:T(8,128)}, f32[512,512]{1,0:T(8,128)}, f32[512,512]{1,0:T(8,128)}) async-done(((f32[512,512]{0,1:T(8,128)}, f32[512,512]{1,0:T(8,128)}, f32[512,512]{1,0:T(8,128)}, f32[512,512]{1,0:T(8,128)}), (f32[512,512]{0,1:T(8,128)}, f32[512,512]{1,0:T(8,128)}, f32[512,512]{1,0:T(8,128)}, ...) | async-done | bytes 4194320 | tf_op jit(solution)/shard_map/psum | solution.py:127
  296.5 8.0 %all-to-all-start.1 = ((bf16[128,4,512]{2,1,0:T(4,128)(2,1)}), bf16[128,4,512]{2,1,0:T(4,128)(2,1)S(1)}, u32[]{:S(2)}, u32[]{:S(2)}) async-start(bf16[128,4,512]{2,1,0:T(4,128)(2,1)} %reshape.45), calls=%async_computation.1 | async-start | bytes 1048576 | tf_op jit(solution)/shard_map/all_to_all | solution.py:82
  304.6 4.3 %convolution_convert_fusion.4 = bf16[2048,512]{1,0:T(8,128)(2,1)} fusion(bf16[2048,512]{0,1:T(8,128)(2,1)} %bitcast.81, bf16[512,512]{1,0:T(8,128)(2,1)} %param.14), kind=kOutput, calls=%fused_computation.37 | convolution fusion | flops 1074790400 | bytes 4718592 | tf_op jit(solution)/shard_map/dot_general | solution.py:67
  308.9 9.2 %all-to-all-done.1 = bf16[128,4,512]{2,1,0:T(4,128)(2,1)S(1)} async-done(((bf16[128,4,512]{2,1,0:T(4,128)(2,1)}), bf16[128,4,512]{2,1,0:T(4,128)(2,1)S(1)}, u32[]{:S(2)}, u32[]{:S(2)}) %all-to-all-start.1) | async-done | bytes 524320 | tf_op jit(solution)/shard_map/all_to_all | solution.py:82
  319.1 52.4 %all-reduce.7.cloned.1.call-done = (f32[512,512]{0,1:T(8,128)}, f32[512,512]{1,0:T(8,128)}, f32[512,512]{1,0:T(8,128)}, f32[512,512]{1,0:T(8,128)}) async-done(((f32[512,512]{0,1:T(8,128)}, f32[512,512]{1,0:T(8,128)}, f32[512,512]{1,0:T(8,128)}, f32[512,512]{1,0:T(8,128)}), (f32[512,512]{0,1:T(8,128)}, f32[512,512]{1,0:T(8,128)}, f32[512,512]{1,0:T(8,128)}, ...) | async-done | bytes 4194320 | tf_op jit(solution)/shard_map/psum | solution.py:126
  371.5 2.6 copy.31
  374.1 2.4 copy.62
  (136 shorter events, 98.8 us)
Async XLA Ops:
  7.2 24.2 %copy-start = (bf16[2048,512]{1,0:T(8,128)(2,1)S(1)}, bf16[2048,512]{1,0:T(8,128)(2,1)}, u32[]{:S(2)}) copy-start(bf16[2048,512]{1,0:T(8,128)(2,1)} %param.10) | copy-start | bytes 6291460
  15.1 12.0 %copy-start.9 = (bf16[512,512]{1,0:T(8,128)(2,1)S(1)}, bf16[512,512]{1,0:T(8,128)(2,1)}, u32[]{:S(2)}) copy-start(bf16[512,512]{1,0:T(8,128)(2,1)} %param.17) | copy-start | bytes 1572868
  15.1 37.6 %all-to-all-start = ((bf16[128,4,1664]{2,1,0:T(4,128)(2,1)}), bf16[128,4,1664]{2,1,0:T(4,128)(2,1)}, u32[]{:S(2)}, u32[]{:S(2)}) async-start(bf16[128,4,1664]{2,1,0:T(4,128)(2,1)} %copy.29), calls=%async_computation | async-start | bytes 3407872 | tf_op jit(solution)/shard_map/all_to_all | solution.py:75
  27.0 265.4 %all-reduce.5.cloned.1.call-start = ((), (), s32[]{:S(2)}) async-start(), calls=%async_computation.2 | async-start | bytes 8388608 | tf_op jit(solution)/shard_map/psum | solution.py:127
  27.1 4.3 %copy-start.10 = (bf16[512,512]{1,0:T(8,128)(2,1)S(1)}, bf16[512,512]{1,0:T(8,128)(2,1)}, u32[]{:S(2)}) copy-start(bf16[512,512]{1,0:T(8,128)(2,1)} %param.14) | copy-start | bytes 1572868
  62.8 1.0 copy-start.6
  62.8 1.8 copy-start.11
  78.0 1.0 copy-start.6
  78.0 1.8 copy-start.11
  93.2 1.0 copy-start.6
  93.2 1.8 copy-start.11
  108.4 1.0 copy-start.6
  108.4 1.8 copy-start.11
  123.6 1.0 copy-start.6
  123.6 1.8 copy-start.11
  138.8 1.0 copy-start.6
  138.8 1.8 copy-start.11
  154.0 1.0 copy-start.6
  154.0 1.8 copy-start.11
  169.2 1.0 copy-start.6
  169.2 1.8 copy-start.11
  181.3 2.7 copy-start.3
  181.3 5.2 %copy-start.8 = (bf16[8,2048,64]{1,2,0:T(8,128)(2,1)S(1)}, bf16[8,2048,64]{1,2,0:T(8,128)(2,1)}, u32[]{:S(2)}) copy-start(bf16[8,2048,64]{1,2,0:T(8,128)(2,1)} %get-tuple-element.66) | copy-start | bytes 6291460
  186.4 2.2 copy-start.7
  192.5 179.0 %all-reduce.7.cloned.1.call-start = ((), (), s32[]{:S(2)}) async-start(), calls=%async_computation.3 | async-start | bytes 8388608 | tf_op jit(solution)/shard_map/psum | solution.py:126
  292.5 1.0 copy-start.2
  293.5 1.6 copy-start.1
  296.5 21.5 %all-to-all-start.1 = ((bf16[128,4,512]{2,1,0:T(4,128)(2,1)}), bf16[128,4,512]{2,1,0:T(4,128)(2,1)S(1)}, u32[]{:S(2)}, u32[]{:S(2)}) async-start(bf16[128,4,512]{2,1,0:T(4,128)(2,1)} %reshape.45), calls=%async_computation.1 | async-start | bytes 1048576 | tf_op jit(solution)/shard_map/all_to_all | solution.py:82
  371.5 5.0 %copy-start.5 = (f32[512,512]{1,0:T(8,128)S(1)}, f32[512,512]{1,0:T(8,128)}, u32[]{:S(2)}) copy-start(f32[512,512]{1,0:T(8,128)} %get-tuple-element.254) | copy-start | bytes 3145732
  374.1 3.3 copy-start.4
Sparse Core Ops, SparseCore 0:
  192.6 99.8 all-reduce.4
  295.1 76.3 all-reduce.6
